TPU v7x, 512 devices: a whole 4x4x16 slice. The times are simulated.
512 devices in a mesh: req: 8 (over z_lo), row: 8 (over x, core), col: 8 (over y, z_hi).
Axes of the slice: x: 4, y: 4, z: 16 (z_hi: 2, z_lo: 8; z = z_hi * 8 + z_lo), core: 2. Of those that a mesh axis runs over, the one named last changes fastest.
Arguments:
- tokens: bfloat16 [1792, 32768], P('col', ('req', 'row')), may hold values from -6 to 6
- qkv_weight: bfloat16 [1792, 2304], P('col', 'row'), may hold values from -0.125 to 0.125
- out_weight: bfloat16 [1792, 1792], P('row', 'col'), may hold values from -0.125 to 0.125
- head_gain: float32 [1792], P('row'), may hold values from 0.1 to 1.9
- prefix_keys: bfloat16 [24, 256, 8192], P('req', 'row', 'col'), may hold values from -6 to 6
- prefix_values: bfloat16 [24, 1792, 8192], P('req', 'row', 'col'), may hold values from -6 to 6
- suffix_len: int32 [64], P(('req', 'col')), may hold values from 1 to 512, 24576 in all
- prefix_owner: int32 [64], P(('req', 'col')), may hold values from 0 to 23
Outputs:
- layer_out: bfloat16 [1792, 32768], P('col', ('req', 'row'))
Inputs may be any that keep to these rules, and one draw needn't show every extreme that they name: `suffix_len`: the longest suffix has exactly 512 live tokens.
All inputs are finite; a program needn't handle non-finite values. No bound on the sum of `suffix_len` on one device may be relied on, other than what follows from the above.
Results may differ from a plain program's by a relative error of at most 0.015.
Values may be sent and summed in bfloat16 or wider, within the bound.
No kernel may reach another device: no remote copies, remote signals or barrier semaphores. Data moves between devices by JAX's collectives and lax.ppermute only.
A program may use at most 64 MiB of HBM per device.

v0:
```python
import jax
import jax.numpy as jnp
from jax import lax
from jax.sharding import PartitionSpec as P

FEAT = 16
SLOTS = 512
HD = 112
epsilon = 1e-05


def feature_map(values_in):
    feature_count = values_in.shape[-1]
    squares = (values_in[..., :, None] * values_in[..., None, :]).reshape(
        values_in.shape[:-1] + (feature_count * feature_count,)
    )
    constant = jnp.ones(values_in.shape[:-1] + (1,), jnp.float32)
    linear = values_in * feature_count ** (-0.25)
    quadratic = squares * (0.5**0.5 / feature_count**0.5)
    return jnp.concatenate([constant, linear, quadratic], axis=-1).astype(jnp.bfloat16)


def feature_columns(values_in):
    feature_count = values_in.shape[-2]
    length = values_in.shape[-1]
    squares = (values_in[..., :, None, :] * values_in[..., None, :, :]).reshape(
        values_in.shape[:-2] + (feature_count * feature_count, length)
    )
    constant = jnp.ones(values_in.shape[:-2] + (1, length), jnp.float32)
    linear = values_in * feature_count ** (-0.25)
    quadratic = squares * (0.5**0.5 / feature_count**0.5)
    return jnp.concatenate([constant, linear, quadratic], axis=-2).astype(jnp.bfloat16)


def shards(
    tokens, qkv_weight, out_weight, head_gain, prefix_keys, prefix_values, suffix_len, prefix_owner
):
    heads_here = head_gain.shape[0] // HD
    partial_proj = lax.dot_general(
        lax.all_gather(tokens, "row", axis=1, tiled=True),
        qkv_weight,
        (((0,), (0,)), ((), ())),
        preferred_element_type=jnp.float32,
    )
    projected = lax.psum_scatter(
        partial_proj.astype(jnp.bfloat16), "col", scatter_dimension=0, tiled=True
    )
    requests = projected.shape[0] // SLOTS
    projected = projected.reshape(requests, SLOTS, heads_here, 2 * FEAT + HD)
    queries = projected[..., :FEAT]
    keys_now = projected[..., FEAT : 2 * FEAT]
    values_now = projected[..., 2 * FEAT :]
    pref_here = prefix_keys.shape[0]
    plen_here = prefix_keys.shape[2]
    feats_cached = feature_columns(
        prefix_keys.reshape(pref_here, heads_here, FEAT, plen_here).astype(jnp.float32)
    )
    values_cached = prefix_values.reshape(pref_here, heads_here, HD, plen_here)
    partial_state = jnp.einsum(
        "phet,phvt->phev", feats_cached, values_cached, preferred_element_type=jnp.float32
    )
    summed_state = lax.psum(partial_state.astype(jnp.bfloat16), "col").astype(jnp.float32)
    states = lax.all_gather(summed_state.astype(jnp.bfloat16), "req", axis=0, tiled=True).astype(
        summed_state.dtype
    )
    prefixes = states.shape[0]
    selector = (prefix_owner[:, None] == jnp.arange(prefixes, dtype=jnp.int32)[None, :]).astype(
        jnp.float32
    )
    chosen = jnp.einsum("rp,phev->rhev", selector, states, precision=lax.Precision.HIGHEST)
    feats_query = feature_map(queries.astype(jnp.float32)).astype(jnp.float32)
    carried = jnp.einsum("rthe,rhev->rthv", feats_query, chosen, precision=lax.Precision.HIGHEST)
    scores = jnp.einsum("rthf,rshf->rhts", queries, keys_now, preferred_element_type=jnp.float32)
    weights = 1.0 + scores * FEAT ** (-0.5) + scores * scores * (0.5 / FEAT)
    positions = jnp.arange(SLOTS, dtype=jnp.int32)
    allowed = (positions[None, None, :] <= positions[None, :, None]) & (
        positions[None, None, :] < suffix_len[:, None, None]
    )
    weights = jnp.where(allowed[:, None], weights, 0.0).astype(jnp.bfloat16)
    within = jnp.einsum("rhts,rshv->rthv", weights, values_now, preferred_element_type=jnp.float32)
    active = (positions[None, :] < suffix_len[:, None])[:, :, None, None]
    attended = jnp.where(active, carried + within, 0.0)
    inverse_rms = lax.rsqrt(jnp.mean(attended * attended, axis=-1, keepdims=True) + epsilon)
    gains = head_gain.reshape(heads_here, HD)
    normed = (
        (attended * inverse_rms * gains)
        .astype(jnp.bfloat16)
        .reshape(requests * SLOTS, heads_here * HD)
    )
    out_terms = lax.dot_general(
        out_weight,
        lax.all_gather(normed, "col", axis=0, tiled=True),
        (((0,), (1,)), ((), ())),
        preferred_element_type=jnp.float32,
    )
    mixed_sums = lax.psum_scatter(
        out_terms.astype(jnp.bfloat16), "row", scatter_dimension=1, tiled=True
    ).astype(jnp.float32)
    return (tokens.astype(jnp.float32) + mixed_sums).astype(jnp.bfloat16)


def solution(mesh):
    in_specs = (
        P("col", ("req", "row")),
        P("col", "row"),
        P("row", "col"),
        P("row"),
        P("req", "row", "col"),
        P("req", "row", "col"),
        P(("req", "col")),
        P(("req", "col")),
    )
    out_specs = P("col", ("req", "row"))
    return jax.shard_map(shards, mesh=mesh, in_specs=in_specs, out_specs=out_specs, check_vma=False)
```

profile of v0, /device:TPU:8, one launch (start us, length us, event | category | flops | bytes accessed | tf_op | source)
XLA Modules:
  0.0 532.3 jit_solution(16961379070519875924)
XLA Ops:
  7.4 1.1 convert.24
  8.4 1.0 multiply_convert_fusion.3
  9.4 0.9 multiply_convert_fusion
  10.3 1.3 fusion.1
  11.7 1.1 copy.20
  12.7 0.0 all-reduce.2.cloned.1.call-update
  12.8 0.0 all-gather.6.cloned.1.call-start
  12.8 0.5 all-gather.6.cloned.1.call-update
  13.3 0.0 all-gather.4.cloned.1.call-start
  13.4 182.7 %all-reduce.2.cloned.1.call-done = bf16[3,2,273,112]{3,1,2,0:T(2,128)(2,1)} async-done(((bf16[3,2,273,112]{3,1,2,0:T(2,128)(2,1)}), bf16[3,2,273,112]{3,1,2,0:T(2,128)(2,1)}) %all-reduce.2.cloned.1.call-update) | async-done | bytes 366928 | tf_op jit(solution)/shard_map/psum | solution.py:62
  196.0 0.0 all-gather.4.cloned.1.call-update
  196.1 0.0 reduce-scatter.3.cloned.1.call-start
  196.1 0.0 all-gather.6.cloned.1.call-done
  196.2 3.7 convolution_convert_fusion
  199.9 0.0 all-gather.8.cloned.1.call-start
  201.2 0.1 mul.133
  201.3 0.1 fusion.17
  201.4 129.0 %all-gather.4.cloned.1.call-done = bf16[24,2,273,112]{3,1,2,0:T(2,128)(2,1)} async-done(((bf16[3,2,273,112]{3,1,2,0:T(2,128)(2,1)}), bf16[24,2,273,112]{3,1,2,0:T(2,128)(2,1)}) %all-gather.4.cloned.1.call-update) | async-done | bytes 2935312 | tf_op jit(solution)/shard_map/all_gather | solution.py:63
  330.4 2.7 fusion.6
  333.2 46.1 %reduce-scatter.3.cloned.1.call-done = bf16[512,288]{0,1:T(8,128)(2,1)} async-done(((bf16[4096,288]{0,1:T(8,128)(2,1)}), bf16[512,288]{0,1:T(8,128)(2,1)}) %reduce-scatter.3.cloned.1.call-update) | async-done | bytes 294928 | tf_op jit(solution)/shard_map/reduce_scatter | solution.py:45
  379.3 0.8 convert_bitcast_fusion
  380.0 0.8 fusion.27
  380.8 1.9 fusion.9
  382.7 0.1 multiply_convert_fusion.1
  382.9 0.8 multiply_reduce_fusion
  383.7 0.8 multiply_convert_fusion.2
  384.5 0.0 reduce-scatter.5.cloned.1.call-start
  384.6 99.5 %all-gather.8.cloned.1.call-done = bf16[4096,224]{0,1:T(8,128)(2,1)} async-done(((bf16[512,224]{0,1:T(8,128)(2,1)}), bf16[4096,224]{0,1:T(8,128)(2,1)}) %all-gather.8.cloned.1.call-update) | async-done | bytes 1835024 | tf_op jit(solution)/shard_map/all_gather | solution.py:92
  484.1 3.4 fusion
  487.6 0.0 reduce-scatter.5.cloned.1.call-update
  487.6 35.6 %reduce-scatter.5.cloned.1.call-done = bf16[224,512]{1,0:T(8,128)(2,1)} async-done(((bf16[224,4096]{1,0:T(8,128)(2,1)}), bf16[224,512]{1,0:T(8,128)(2,1)}) %reduce-scatter.5.cloned.1.call-update) | async-done | bytes 229392 | tf_op jit(solution)/shard_map/reduce_scatter | solution.py:96
  523.2 1.7 add_convert_fusion
  (16 shorter events, 0.1 us)
Async XLA Ops:
  7.4 3.0 copy-start
  7.4 188.7 %all-reduce.2.cloned.1.call-start = ((), (), s32[]{:S(2)}) async-start(), calls=%async_computation.2 | async-start | bytes 838656 | tf_op jit(solution)/shard_map/psum | solution.py:62
  10.3 185.8 %copy-start.2 = (bf16[224,288]{0,1:T(8,128)(2,1)S(1)}, bf16[224,288]{0,1:T(8,128)(2,1)}, u32[]{:S(2)}) copy-start(bf16[224,288]{0,1:T(8,128)(2,1)} %param.9) | copy-start | bytes 387076
  12.8 183.4 %all-gather.6.cloned.1.call-start = ((), (), s32[]{:S(2)}) async-start(), calls=%async_computation.4 | async-start | bytes 2064384 | tf_op jit(solution)/shard_map/all_gather | solution.py:40
  13.3 317.1 %all-gather.4.cloned.1.call-start = ((), (), s32[]{:S(2)}) async-start(), calls=%async_computation.3 | async-start | bytes 3773952 | tf_op jit(solution)/shard_map/all_gather | solution.py:63
  196.1 183.2 %reduce-scatter.3.cloned.1.call-start = ((), (), s32[]{:S(2)}) async-start(), calls=%async_computation.5 | async-start | bytes 2654208 | tf_op jit(solution)/shard_map/reduce_scatter | solution.py:45
  199.9 1.4 copy-start.4
  199.9 284.2 %all-gather.8.cloned.1.call-start = ((), (), s32[]{:S(2)}) async-start(), calls=%async_computation.6 | async-start | bytes 2064384 | tf_op jit(solution)/shard_map/all_gather | solution.py:92
  382.7 101.4 %copy-start.3 = (bf16[224,224]{1,0:T(8,128)(2,1)S(1)}, bf16[224,224]{1,0:T(8,128)(2,1)}, u32[]{:S(2)}) copy-start(bf16[224,224]{1,0:T(8,128)(2,1)} %param.10) | copy-start | bytes 301060
  384.5 138.7 %copy-start.1 = (bf16[224,512]{1,0:T(8,128)(2,1)S(1)}, bf16[224,512]{1,0:T(8,128)(2,1)}, u32[]{:S(2)}) copy-start(bf16[224,512]{1,0:T(8,128)(2,1)} %param.8) | copy-start | bytes 688132
  384.5 138.7 %reduce-scatter.5.cloned.1.call-start = ((), (), s32[]{:S(2)}) async-start(), calls=%async_computation.7 | async-start | bytes 2064384 | tf_op jit(solution)/shard_map/reduce_scatter | solution.py:96
Sparse Core Ops, SparseCore 0:
  12.9 183.1 all-reduce.1
  201.6 177.6 reduce-scatter.2
  384.6 99.4 all-gather.7
Sparse Core Ops, SparseCore 1:
  15.4 36.7 all-gather.5
  196.1 134.2 all-gather.3
  487.7 35.5 reduce-scatter.4
where the time goes:
time: 533 us; the launch traced here: 532 us
  waiting for transfers between devices  494 us (93%)
  between operations  16.2 us (3%)
  matrix products  13.9 us (3%)
  other arithmetic  7.12 us (1%)
    psum x1, waiting for transfers between devices, shards(): lax.psum(partial_state.astype(jnp.bfloat16), 'col').astype(jnp.float32)  183 us
    all_gather x1, waiting for transfers between devices, shards(): lax.all_gather(summed_state.astype(jnp.bfloat16), 'req', axis=0, tiled=True)  129 us
    all_gather x1, waiting for transfers between devices, shards(): lax.all_gather(normed, 'col', axis=0, tiled=True)  99.5 us
    reduce_scatter x1, waiting for transfers between devices, shards(): lax.psum_scatter(partial_proj.astype(jnp.bfloat16), 'col', scatter_dimens...  46.1 us
    reduce_scatter x1, waiting for transfers between devices, shards(): lax.psum_scatter(out_terms.astype(jnp.bfloat16), 'row', scatter_dimension...  35.6 us
  transfers between devices with their start and end apart: 6, of which 5 were waited for; matrix products, arithmetic and copies ran while one was open for 1% of the time, Pallas kernels for 0%

commit v1 on v0

--- a/solution.py
+++ b/solution.py
@@ -7,6 +7,11 @@
 SLOTS = 512
 HD = 112
 epsilon = 1e-05
+
+
+def recover_sites(load, mesh_dim="col"):
+    local_out = jnp.sum(lax.all_gather(load, mesh_dim), 0)
+    return local_out
 
 
 def feature_map(values_in):
@@ -59,7 +64,7 @@
     partial_state = jnp.einsum(
         "phet,phvt->phev", feats_cached, values_cached, preferred_element_type=jnp.float32
     )
-    summed_state = lax.psum(partial_state.astype(jnp.bfloat16), "col").astype(jnp.float32)
+    summed_state = recover_sites(partial_state.astype(jnp.bfloat16)).astype(jnp.float32)
     states = lax.all_gather(summed_state.astype(jnp.bfloat16), "req", axis=0, tiled=True).astype(
         summed_state.dtype
     )

time: 533 us -> 597 us (1.12)
  waiting for transfers between devices: 494 us -> 553 us
  other arithmetic: 7.12 us -> 13.9 us
    psum x1 -> x0, waiting for transfers between devices: 183 us -> none  [shards(): lax.psum(partial_state.astype(jnp.bfloat16), 'col').astype(jnp.float32)]
    all_gather x0 -> x1, waiting for transfers between devices: none -> 152 us  [recover_sites(): local_out = jnp.sum(lax.all_gather(load, mesh_dim), 0)]
    reduce_scatter x1, waiting for transfers between devices: 46.1 us -> 150 us  [shards(): lax.psum_scatter(partial_proj.astype(jnp.bfloat16), 'col', scatter_dimens...]
    all_gather x1, waiting for transfers between devices: 129 us -> 77.3 us  [shards(): lax.all_gather(summed_state.astype(jnp.bfloat16), 'req', axis=0, tiled=True)]
    all_gather x1, waiting for transfers between devices: 0.03 us -> 33.8 us  [shards(): lax.all_gather(tokens, 'row', axis=1, tiled=True)]
    reduce_sum x0 -> x1, other arithmetic: none -> 6.87 us  [recover_sites(): local_out = jnp.sum(lax.all_gather(load, mesh_dim), 0)]
  transfers between devices with their start and end apart: 6 -> 6, of which waited for: 5 -> 6; matrix products, arithmetic and copies ran while one was open for 1% -> 3% of each run, Pallas kernels for 0% -> 0%
where the time goes in v1:
time: 597 us
  waiting for transfers between devices  553 us (93%)
  between operations  14.9 us (2%)
  other arithmetic  13.9 us (2%)
  matrix products  13.9 us (2%)
    all_gather x1, waiting for transfers between devices, recover_sites(): local_out = jnp.sum(lax.all_gather(load, mesh_dim), 0)  152 us
    reduce_scatter x1, waiting for transfers between devices, shards(): lax.psum_scatter(partial_proj.astype(jnp.bfloat16), 'col', scatter_dimens...  150 us
    all_gather x1, waiting for transfers between devices, shards(): lax.all_gather(normed, 'col', axis=0, tiled=True)  103 us
    all_gather x1, waiting for transfers between devices, shards(): lax.all_gather(summed_state.astype(jnp.bfloat16), 'req', axis=0, tiled=True)  77.3 us
    reduce_scatter x1, waiting for transfers between devices, shards(): lax.psum_scatter(out_terms.astype(jnp.bfloat16), 'row', scatter_dimension...  35.8 us
    all_gather x1, waiting for transfers between devices, shards(): lax.all_gather(tokens, 'row', axis=1, tiled=True)  33.8 us
  transfers between devices with their start and end apart: 6, of which 6 were waited for; matrix products, arithmetic and copies ran while one was open for 3% of the time, Pallas kernels for 0%

profile of v1, /device:TPU:8, one launch (start us, length us, event | category | flops | bytes accessed | tf_op | source)
XLA Modules:
  0.0 596.8 jit_solution(17926042103733562626)
XLA Ops:
  6.5 0.7 all-gather.8.cloned.1.call-update
  7.3 0.0 all-gather.12.cloned.1.call-start
  7.3 1.0 convert.25
  8.3 1.0 multiply_convert_fusion.3
  9.2 0.9 multiply_convert_fusion
  10.2 1.3 fusion.10
  11.5 1.1 copy.9
  12.6 0.0 reduce-scatter.3.cloned.1.call-start
  12.6 33.8 %all-gather.8.cloned.1.call-done = bf16[224,4096]{1,0:T(8,128)(2,1)} async-done(((bf16[224,512]{1,0:T(8,128)(2,1)}), bf16[224,4096]{1,0:T(8,128)(2,1)}) %all-gather.8.cloned.1.call-update) | async-done | bytes 1835024 | tf_op jit(solution)/shard_map/all_gather | solution.py:45
  46.4 3.7 convolution_convert_fusion
  50.1 0.0 reduce-scatter.3.cloned.1.call-update
  50.1 0.0 all-gather.6.cloned.1.call-start
  50.2 152.4 %all-gather.12.cloned.1.call-done = bf16[24,2,273,112]{3,1,2,0:T(2,128)(2,1)} async-done(((bf16[3,2,273,112]{3,1,2,0:T(2,128)(2,1)}), bf16[24,2,273,112]{3,1,2,0:T(2,128)(2,1)}) %all-gather.12.cloned.1.call-update) | async-done | bytes 2935312 | tf_op jit(solution)/shard_map/all_gather | solution.py:13
  202.5 6.9 %reduce_sum.21 = bf16[3,2,273,112]{3,1,2,0:T(2,128)(2,1)} reduce(bf16[8,3,2,273,112]{4,2,3,1,0:T(2,128)(2,1)} %bitcast.55, bf16[]{:T(256)} %constant.4.clone.1), dimensions={0}, to_apply=%region_0.0 | reduce | flops 1284192 | bytes 3302210 | tf_op jit(solution)/shard_map/reduce_sum | solution.py:13
  209.4 0.0 all-gather.6.cloned.1.call-update
  209.4 0.0 all-gather.10.cloned.1.call-start
  210.8 0.1 mul.133
  210.9 0.1 fusion.20
  210.9 149.8 %reduce-scatter.3.cloned.1.call-done = bf16[512,288]{0,1:T(8,128)(2,1)} async-done(((bf16[4096,288]{0,1:T(8,128)(2,1)}), bf16[512,288]{0,1:T(8,128)(2,1)}) %reduce-scatter.3.cloned.1.call-update) | async-done | bytes 294928 | tf_op jit(solution)/shard_map/reduce_scatter | solution.py:50
  360.7 0.8 fusion.30
  361.5 0.8 convert_bitcast_fusion
  362.3 0.1 multiply_convert_fusion.1
  362.4 1.9 fusion.9
  364.3 77.3 %all-gather.6.cloned.1.call-done = bf16[24,2,273,112]{3,1,2,0:T(2,128)(2,1)} async-done(((bf16[3,2,273,112]{3,1,2,0:T(2,128)(2,1)}), bf16[24,2,273,112]{3,1,2,0:T(2,128)(2,1)}) %all-gather.6.cloned.1.call-update) | async-done | bytes 2935312 | tf_op jit(solution)/shard_map/all_gather | solution.py:68
  441.6 2.7 fusion.6
  444.3 0.8 multiply_reduce_fusion
  445.2 0.8 multiply_convert_fusion.2
  446.0 0.0 reduce-scatter.5.cloned.1.call-start
  446.1 103.0 %all-gather.10.cloned.1.call-done = bf16[4096,224]{0,1:T(8,128)(2,1)} async-done(((bf16[512,224]{0,1:T(8,128)(2,1)}), bf16[4096,224]{0,1:T(8,128)(2,1)}) %all-gather.10.cloned.1.call-update) | async-done | bytes 1835024 | tf_op jit(solution)/shard_map/all_gather | solution.py:97
  549.1 3.4 fusion
  552.5 35.8 %reduce-scatter.5.cloned.1.call-done = bf16[224,512]{1,0:T(8,128)(2,1)} async-done(((bf16[224,4096]{1,0:T(8,128)(2,1)}), bf16[224,512]{1,0:T(8,128)(2,1)}) %reduce-scatter.5.cloned.1.call-update) | async-done | bytes 229392 | tf_op jit(solution)/shard_map/reduce_scatter | solution.py:101
  588.3 1.7 add_convert_fusion
  (17 shorter events, 0.1 us)
Async XLA Ops:
  6.5 3.6 copy-start
  6.5 39.9 %all-gather.8.cloned.1.call-start = ((), (), s32[]{:S(2)}) async-start(), calls=%async_computation.3 | async-start | bytes 2064384 | tf_op jit(solution)/shard_map/all_gather | solution.py:45
  7.3 195.3 %all-gather.12.cloned.1.call-start = ((), (), s32[]{:S(2)}) async-start(), calls=%async_computation.7 | async-start | bytes 3773952 | tf_op jit(solution)/shard_map/all_gather | solution.py:13
  10.2 36.2 %copy-start.2 = (bf16[224,288]{0,1:T(8,128)(2,1)S(1)}, bf16[224,288]{0,1:T(8,128)(2,1)}, u32[]{:S(2)}) copy-start(bf16[224,288]{0,1:T(8,128)(2,1)} %param.9) | copy-start | bytes 387076
  12.6 348.2 %reduce-scatter.3.cloned.1.call-start = ((), (), s32[]{:S(2)}) async-start(), calls=%async_computation.4 | async-start | bytes 2654208 | tf_op jit(solution)/shard_map/reduce_scatter | solution.py:50
  50.1 391.5 %all-gather.6.cloned.1.call-start = ((), (), s32[]{:S(2)}) async-start(), calls=%async_computation.2 | async-start | bytes 3773952 | tf_op jit(solution)/shard_map/all_gather | solution.py:68
  202.5 8.2 %copy-start.4 = (f32[224]{0:T(256)S(1)}, f32[224]{0:T(256)}, u32[]{:S(2)}) copy-start(f32[224]{0:T(256)} %param.11) | copy-start | bytes 2692
  209.4 339.6 %all-gather.10.cloned.1.call-start = ((), (), s32[]{:S(2)}) async-start(), calls=%async_computation.5 | async-start | bytes 2064384 | tf_op jit(solution)/shard_map/all_gather | solution.py:97
  444.3 104.7 %copy-start.3 = (bf16[224,224]{1,0:T(8,128)(2,1)S(1)}, bf16[224,224]{1,0:T(8,128)(2,1)}, u32[]{:S(2)}) copy-start(bf16[224,224]{1,0:T(8,128)(2,1)} %param.10) | copy-start | bytes 301060
  446.0 142.3 %copy-start.1 = (bf16[224,512]{1,0:T(8,128)(2,1)S(1)}, bf16[224,512]{1,0:T(8,128)(2,1)}, u32[]{:S(2)}) copy-start(bf16[224,512]{1,0:T(8,128)(2,1)} %param.8) | copy-start | bytes 688132
  446.0 142.3 %reduce-scatter.5.cloned.1.call-start = ((), (), s32[]{:S(2)}) async-start(), calls=%async_computation.6 | async-start | bytes 2064384 | tf_op jit(solution)/shard_map/reduce_scatter | solution.py:101
Sparse Core Ops, SparseCore 0:
  9.5 36.8 all-gather.7
  49.6 152.8 all-gather.11
  207.2 153.4 reduce-scatter.2
  362.7 78.8 all-gather.5
  446.1 102.8 all-gather.9
  552.6 35.5 reduce-scatter.4
